TPU v7x, 256 devices: a whole 4x4x8 slice. The times are simulated.
256 devices in a mesh: dp: 16 (over x_hi, y, core), block: 16 (over z, x_lo).
Axes of the slice: x: 4 (x_hi: 2, x_lo: 2; x = x_hi * 2 + x_lo), y: 4, z: 8, core: 2. Of those that a mesh axis runs over, the one named last changes fastest.
Arguments:
- inputs: bfloat16 [128, 128, 32768], P('block', None, 'dp'), may hold values from -6 to 6
- left_factor: bfloat16 [128, 128, 128], P('block'), may hold values from -0.5 to 0.5
- right_factor: bfloat16 [128, 128, 128], P('block'), may hold values from -0.5 to 0.5
- cotangent: bfloat16 [128, 128, 32768], P('block', None, 'dp'), may hold values from -6 to 6
Outputs:
- input_grad: bfloat16 [128, 128, 32768], P('block', None, 'dp')
- left_grad: float32 [128, 128, 128], P('block', 'dp')
- right_grad: float32 [128, 128, 128], P('block', 'dp')
All inputs are finite; a program needn't handle non-finite values.
Results may differ from a plain program's by a relative error of at most 0.0055.
Values may be sent and summed in bfloat16 or wider, within the bound.
No kernel may reach another device: no remote copies, remote signals or barrier semaphores. Data moves between devices by JAX's collectives and lax.ppermute only.
A program may use at most 128 MiB of HBM per device.

v0:
```python
import jax
import jax.numpy as jnp
from jax import lax
from jax.sharding import PartitionSpec as P

MICRO = 2


def gelu_slope(values):
    return jax.vjp(jax.nn.gelu, values)[1](jnp.ones_like(values))[0]


def local(inputs, left_factor, right_factor, cotangent):
    tokens_local = inputs.shape[2]
    scale = float(lax.axis_size("dp") * tokens_local) ** (-0.5)
    groups = MICRO
    group_width = tokens_local // groups
    input_pieces = []
    grad_left = None
    grad_right = None
    for group in range(groups):
        x_group = inputs[:, :, group * group_width : (group + 1) * group_width]
        dy_group = cotangent[:, :, group * group_width : (group + 1) * group_width]
        outgoing = jnp.einsum(
            "ict,ico->oit", x_group, left_factor, preferred_element_type=jnp.float32
        ).astype(jnp.bfloat16)
        forward_received = lax.all_to_all(
            outgoing, "block", split_axis=0, concat_axis=1, tiled=True
        )
        mixed = jnp.einsum(
            "jit,jik->jkt", forward_received, right_factor, preferred_element_type=jnp.float32
        )
        slope = gelu_slope(mixed)
        mixed_grad = (dy_group.astype(jnp.float32) * slope).astype(jnp.bfloat16)
        right_term = (
            jnp.einsum(
                "jit,jkt->jik", forward_received, mixed_grad, preferred_element_type=jnp.float32
            )
            * scale
        )
        permuted_grad = jnp.einsum(
            "jkt,jik->jit", mixed_grad, right_factor, preferred_element_type=jnp.float32
        ).astype(jnp.bfloat16)
        received = lax.all_to_all(permuted_grad, "block", split_axis=1, concat_axis=0, tiled=True)
        branch = jnp.einsum(
            "oit,ico->ict", received, left_factor, preferred_element_type=jnp.float32
        )
        residual = dy_group.astype(jnp.float32)
        input_pieces.append((residual + branch).astype(jnp.bfloat16))
        left_term = (
            jnp.einsum("ict,oit->ico", x_group, received, preferred_element_type=jnp.float32)
            * scale
        )
        left_part, right_part = (
            lax.psum_scatter(left_term, "dp", scatter_dimension=1, tiled=True),
            lax.psum_scatter(right_term, "dp", scatter_dimension=1, tiled=True),
        )
        grad_left = left_part if grad_left is None else grad_left + left_part
        grad_right = right_part if grad_right is None else grad_right + right_part
    input_grad = jnp.concatenate(input_pieces, axis=2)
    return (input_grad, grad_left, grad_right)


def solution(mesh):
    placed = (
        P("block", None, "dp"),
        P("block", None, None),
        P("block", None, None),
        P("block", None, "dp"),
    )
    return jax.shard_map(
        local,
        mesh=mesh,
        in_specs=placed,
        out_specs=(P("block", None, "dp"), P("block", "dp", None), P("block", "dp", None)),
        check_vma=False,
    )
```

profile of v0, /device:TPU:1, one launch (start us, length us, event | category | flops | bytes accessed | tf_op | source)
XLA Modules:
  0.0 398.4 jit_solution(1010243307833431431)
XLA Ops:
  12.1 10.2 %all-to-all-start.2 = ((bf16[128,8,1024]{2,1,0:T(8,128)(2,1)}), bf16[128,8,1024]{2,1,0:T(8,128)(2,1)}, u32[]{:S(2)}, u32[]{:S(2)}) async-start(bf16[128,8,1024]{2,1,0:T(8,128)(2,1)} %copy.77), calls=%async_computation.2 | async-start | bytes 4194304 | tf_op jit(solution)/shard_map/all_to_all | solution.py:27
  27.2 43.6 %all-to-all-done.2 = bf16[128,8,1024]{2,1,0:T(8,128)(2,1)} async-done(((bf16[128,8,1024]{2,1,0:T(8,128)(2,1)}), bf16[128,8,1024]{2,1,0:T(8,128)(2,1)}, u32[]{:S(2)}, u32[]{:S(2)}) %all-to-all-start.2) | async-done | bytes 2097184 | tf_op jit(solution)/shard_map/all_to_all | solution.py:27
  70.9 5.7 %all-to-all-start = ((bf16[128,8,1024]{2,1,0:T(8,128)(2,1)}), bf16[128,8,1024]{2,1,0:T(8,128)(2,1)}, u32[]{:S(2)}, u32[]{:S(2)}) async-start(bf16[128,8,1024]{2,1,0:T(8,128)(2,1)} %copy.68), calls=%async_computation | async-start | bytes 4194304 | tf_op jit(solution)/shard_map/all_to_all | solution.py:27
  76.6 4.9 %fusion.59 = (bf16[8,128,1024]{2,1,0:T(8,128)(2,1)}, bf16[8,128,1024]{2,1,0:T(8,128)(2,1)}) fusion(bf16[8,128,2048]{2,1,0:T(8,128)(2,1)} %param.7), kind=kLoop, calls=%fused_computation.58 | loop fusion | bytes 8388608 | tf_op jit(solution)/shard_map/slice | solution.py:23
  81.5 3.0 copy.100
  84.5 5.0 %fusion.2 = bf16[8,128,1024]{1,2,0:T(8,128)(2,1)S(1)} fusion(bf16[8,128,1024]{1,2,0:T(8,128)(2,1)S(1)} %copy.100, bf16[8,128,128]{2,1,0:T(8,128)(2,1)S(1)} %copy-done, bf16[8,16,8,1024]{3,2,0,1:T(8,128)(2,1)} %bitcast.13), kind=kOutput, calls=%fused_computation.10 | convolution fusion | flops 289406976 | bytes 6553600 | tf_op jit(solution)/shard_map/jit,jik->jkt/dot_general | solution.py:30
  93.0 4.2 %copy.80 = bf16[8,128,1024]{2,0,1:T(8,128)(2,1)} copy(bf16[8,128,1024]{1,2,0:T(8,128)(2,1)} %convert_bitcast_fusion) | data formatting | bytes 4194304 | tf_op jit(solution)/shard_map/convert_element_type | solution.py:43
  97.2 27.6 %all-to-all-done = bf16[128,8,1024]{2,1,0:T(8,128)(2,1)} async-done(((bf16[128,8,1024]{2,1,0:T(8,128)(2,1)}), bf16[128,8,1024]{2,1,0:T(8,128)(2,1)}, u32[]{:S(2)}, u32[]{:S(2)}) %all-to-all-start) | async-done | bytes 2097184 | tf_op jit(solution)/shard_map/all_to_all | solution.py:27
  124.8 6.1 %all-to-all-start.3 = ((bf16[8,128,1024]{2,0,1:T(8,128)(2,1)}), bf16[8,128,1024]{2,0,1:T(8,128)(2,1)}, u32[]{:S(2)}, u32[]{:S(2)}) async-start(bf16[8,128,1024]{2,0,1:T(8,128)(2,1)} %copy.80), calls=%async_computation.3 | async-start | bytes 4194304 | tf_op jit(solution)/shard_map/all_to_all | solution.py:44
  130.9 4.0 copy.99
  134.8 5.7 %fusion = bf16[8,128,1024]{1,2,0:T(8,128)(2,1)S(1)} fusion(bf16[8,128,1024]{1,2,0:T(8,128)(2,1)} %copy.99, bf16[8,128,128]{2,1,0:T(8,128)(2,1)S(1)} %copy-done, bf16[8,16,8,1024]{3,2,0,1:T(8,128)(2,1)} %bitcast.2), kind=kOutput, calls=%fused_computation.8 | convolution fusion | flops 289406976 | bytes 6553600 | tf_op jit(solution)/shard_map/jit,jik->jkt/dot_general | solution.py:30
  143.9 4.2 %copy.71 = bf16[8,128,1024]{2,0,1:T(8,128)(2,1)} copy(bf16[8,128,1024]{1,2,0:T(8,128)(2,1)} %convert_bitcast_fusion.2) | data formatting | bytes 4194304 | tf_op jit(solution)/shard_map/convert_element_type | solution.py:43
  148.1 30.9 %all-to-all-done.3 = bf16[8,128,1024]{2,0,1:T(8,128)(2,1)} async-done(((bf16[8,128,1024]{2,0,1:T(8,128)(2,1)}), bf16[8,128,1024]{2,0,1:T(8,128)(2,1)}, u32[]{:S(2)}, u32[]{:S(2)}) %all-to-all-start.3) | async-done | bytes 2097184 | tf_op jit(solution)/shard_map/all_to_all | solution.py:44
  179.0 6.1 %all-to-all-start.1 = ((bf16[8,128,1024]{2,0,1:T(8,128)(2,1)}), bf16[8,128,1024]{2,0,1:T(8,128)(2,1)}, u32[]{:S(2)}, u32[]{:S(2)}) async-start(bf16[8,128,1024]{2,0,1:T(8,128)(2,1)} %copy.71), calls=%async_computation.1 | async-start | bytes 4194304 | tf_op jit(solution)/shard_map/all_to_all | solution.py:44
  185.1 3.2 copy.82
  192.0 41.3 %all-to-all-done.1 = bf16[8,128,1024]{2,0,1:T(8,128)(2,1)} async-done(((bf16[8,128,1024]{2,0,1:T(8,128)(2,1)}), bf16[8,128,1024]{2,0,1:T(8,128)(2,1)}, u32[]{:S(2)}, u32[]{:S(2)}) %all-to-all-start.1) | async-done | bytes 2097184 | tf_op jit(solution)/shard_map/all_to_all | solution.py:44
  233.2 3.2 copy.73
  237.7 3.7 fusion.54
  242.8 3.1 fusion.18
  245.9 3.1 fusion.41
  249.1 4.1 %fusion.3 = bf16[8,128,1024]{1,2,0:T(8,128)(2,1)S(1)} fusion(bf16[8,128,1024]{1,2,0:T(8,128)(2,1)S(1)} %copy.100, bf16[8,128,128]{2,1,0:T(8,128)(2,1)S(1)} %copy-done.5, bf16[128,8,1024]{2,1,0:T(8,128)(2,1)} %bitcast.75), kind=kOutput, calls=%fused_computation.11 | convolution fusion | flops 271581184 | bytes 6553600 | tf_op jit(solution)/shard_map/oit,ico->ict/dot_general | solution.py:45
  257.8 6.5 %copy.89 = bf16[8,128,2048]{2,1,0:T(8,128)(2,1)} copy(bf16[8,128,2048]{1,2,0:T(8,128)(2,1)} %pad_maximum_fusion) | data formatting | bytes 8388608
  264.3 50.1 %reduce-scatter.3.cloned.1.call-done = f32[8,8,128]{2,0,1:T(8,128)} async-done(((f32[8,128,128]{2,0,1:T(8,128)}), f32[8,8,128]{2,0,1:T(8,128)}) %reduce-scatter.3.cloned.1.call-update) | async-done | bytes 32784 | tf_op jit(solution)/shard_map/reduce_scatter | solution.py:55
  315.8 75.8 %reduce-scatter.5.cloned.1.call-done = f32[8,8,128]{2,1,0:T(8,128)} async-done(((f32[8,128,128]{2,1,0:T(8,128)}), f32[8,8,128]{2,1,0:T(8,128)}) %reduce-scatter.5.cloned.1.call-update) | async-done | bytes 32784 | tf_op jit(solution)/shard_map/reduce_scatter | solution.py:56
  (37 shorter events, 29.0 us)
Async XLA Ops:
  7.2 77.3 %copy-start = (bf16[8,128,128]{2,1,0:T(8,128)(2,1)S(1)}, bf16[8,128,128]{2,1,0:T(8,128)(2,1)}, u32[]{:S(2)}) copy-start(bf16[8,128,128]{2,1,0:T(8,128)(2,1)} %param.6) | copy-start | bytes 786436
  12.1 10.2 %copy-start.5 = (bf16[8,128,128]{2,1,0:T(8,128)(2,1)S(1)}, bf16[8,128,128]{2,1,0:T(8,128)(2,1)}, u32[]{:S(2)}) copy-start(bf16[8,128,128]{2,1,0:T(8,128)(2,1)} %param.5) | copy-start | bytes 786436
  12.1 58.7 %all-to-all-start.2 = ((bf16[128,8,1024]{2,1,0:T(8,128)(2,1)}), bf16[128,8,1024]{2,1,0:T(8,128)(2,1)}, u32[]{:S(2)}, u32[]{:S(2)}) async-start(bf16[128,8,1024]{2,1,0:T(8,128)(2,1)} %copy.77), calls=%async_computation.2 | async-start | bytes 4194304 | tf_op jit(solution)/shard_map/all_to_all | solution.py:27
  70.9 53.9 %all-to-all-start = ((bf16[128,8,1024]{2,1,0:T(8,128)(2,1)}), bf16[128,8,1024]{2,1,0:T(8,128)(2,1)}, u32[]{:S(2)}, u32[]{:S(2)}) async-start(bf16[128,8,1024]{2,1,0:T(8,128)(2,1)} %copy.68), calls=%async_computation | async-start | bytes 4194304 | tf_op jit(solution)/shard_map/all_to_all | solution.py:27
  89.6 1.4 copy-start.8
  124.8 54.2 %all-to-all-start.3 = ((bf16[8,128,1024]{2,0,1:T(8,128)(2,1)}), bf16[8,128,1024]{2,0,1:T(8,128)(2,1)}, u32[]{:S(2)}, u32[]{:S(2)}) async-start(bf16[8,128,1024]{2,0,1:T(8,128)(2,1)} %copy.80), calls=%async_computation.3 | async-start | bytes 4194304 | tf_op jit(solution)/shard_map/all_to_all | solution.py:44
  140.5 1.4 copy-start.9
  179.0 54.2 %all-to-all-start.1 = ((bf16[8,128,1024]{2,0,1:T(8,128)(2,1)}), bf16[8,128,1024]{2,0,1:T(8,128)(2,1)}, u32[]{:S(2)}, u32[]{:S(2)}) async-start(bf16[8,128,1024]{2,0,1:T(8,128)(2,1)} %copy.71), calls=%async_computation.1 | async-start | bytes 4194304 | tf_op jit(solution)/shard_map/all_to_all | solution.py:44
  185.1 129.3 %reduce-scatter.3.cloned.1.call-start = ((), (), s32[]{:S(2)}) async-start(), calls=%async_computation.6 | async-start | bytes 557056 | tf_op jit(solution)/shard_map/reduce_scatter | solution.py:55
  185.1 4.5 %copy-start.6 = (bf16[8,128,2048]{2,1,0:T(8,128)(2,1)S(1)}, bf16[8,128,2048]{2,1,0:T(8,128)(2,1)}, u32[]{:S(2)}) copy-start(bf16[8,128,2048]{2,1,0:T(8,128)(2,1)} %param.4) | copy-start | bytes 12582916
  188.3 1.3 copy-start.2
  233.2 4.5 %copy-start.7 = (bf16[8,128,2048]{2,1,0:T(8,128)(2,1)S(1)}, bf16[8,128,2048]{2,1,0:T(8,128)(2,1)}, u32[]{:S(2)}) copy-start(bf16[8,128,2048]{2,1,0:T(8,128)(2,1)} %param.4) | copy-start | bytes 12582916
  236.4 1.3 copy-start.3
  242.5 149.0 %reduce-scatter.5.cloned.1.call-start = ((), (), s32[]{:S(2)}) async-start(), calls=%async_computation.7 | async-start | bytes 557056 | tf_op jit(solution)/shard_map/reduce_scatter | solution.py:56
  242.8 3.1 copy-start.10
  249.0 4.2 %copy-start.1 = (bf16[8,128,1024]{1,2,0:T(8,128)(2,1)S(1)}, bf16[8,128,1024]{1,2,0:T(8,128)(2,1)}, u32[]{:S(2)}) copy-start(bf16[8,128,1024]{1,2,0:T(8,128)(2,1)} %copy.99) | copy-start | bytes 6291460
  249.1 4.2 %copy-start.4 = (bf16[16,8,8,1024]{3,2,1,0:T(8,128)(2,1)S(1)}, bf16[16,8,8,1024]{3,2,1,0:T(8,128)(2,1)}, u32[]{:S(2)}) copy-start(bf16[16,8,8,1024]{3,2,1,0:T(8,128)(2,1)} %copy-done.3) | copy-start | bytes 6291460
Sparse Core Ops, SparseCore 0:
  242.6 71.7 reduce-scatter.2
  318.9 72.5 reduce-scatter.4
where the time goes:
time: 400 us; the launch traced here: 398 us
  waiting for transfers between devices  269 us (67%)
  local copies, waits for them, and re-layouts  45.8 us (11%)
  matrix products  38.4 us (10%)
  starting transfers between devices  28.4 us (7%)
  between operations  14.3 us (4%)
    reduce_scatter x1, waiting for transfers between devices, local(): lax.psum_scatter(right_term, 'dp', scatter_dimension=1, tiled=True)  75.8 us
    all_to_all x2, waiting for transfers between devices, local(): lax.all_to_all(permuted_grad, 'block', split_axis=1, concat_axis=0, tiled...  72.2 us
    all_to_all x2, waiting for transfers between devices, local(): lax.all_to_all(outgoing, 'block', split_axis=0, concat_axis=1, tiled=True)  71.2 us
    reduce_scatter x1, waiting for transfers between devices, local(): lax.psum_scatter(left_term, 'dp', scatter_dimension=1, tiled=True)  50.1 us
    unnamed x26, local copies, waits for them, and re-layouts  20.2 us
    all_to_all x2, starting transfers between devices, local(): lax.all_to_all(outgoing, 'block', split_axis=0, concat_axis=1, tiled=True)  16 us
    all_to_all x2, starting transfers between devices, local(): lax.all_to_all(permuted_grad, 'block', split_axis=1, concat_axis=0, tiled...  12.1 us
    dot_general x2, matrix products, local(): jnp.einsum('jit,jik->jkt', forward_received, right_factor, preferred_elem...  10.7 us
  transfers between devices with their start and end apart: 6, of which 6 were waited for; matrix products, arithmetic and copies ran while one was open for 17% of the time, Pallas kernels for 0%

commit v1 on v0

--- a/solution.py
+++ b/solution.py
@@ -8,6 +8,13 @@
 
 def gelu_slope(values):
     return jax.vjp(jax.nn.gelu, values)[1](jnp.ones_like(values))[0]
+
+
+def dp_reduce_scatter(terms):
+    n_dp = lax.axis_size("dp")
+    received = lax.all_to_all(terms, "dp", split_axis=2, concat_axis=0, tiled=True)
+    received = received.reshape((n_dp,) + terms.shape[:2] + (terms.shape[2] // n_dp,) + terms.shape[3:])
+    return jnp.sum(received, axis=0)
 
 
 def local(inputs, left_factor, right_factor, cotangent):
@@ -51,14 +58,11 @@
             jnp.einsum("ict,oit->ico", x_group, received, preferred_element_type=jnp.float32)
             * scale
         )
-        left_part, right_part = (
-            lax.psum_scatter(left_term, "dp", scatter_dimension=1, tiled=True),
-            lax.psum_scatter(right_term, "dp", scatter_dimension=1, tiled=True),
-        )
-        grad_left = left_part if grad_left is None else grad_left + left_part
-        grad_right = right_part if grad_right is None else grad_right + right_part
+        grad_left = left_term if grad_left is None else grad_left + left_term
+        grad_right = right_term if grad_right is None else grad_right + right_term
     input_grad = jnp.concatenate(input_pieces, axis=2)
-    return (input_grad, grad_left, grad_right)
+    reduced = dp_reduce_scatter(jnp.stack([grad_left, grad_right]))
+    return (input_grad, reduced[0], reduced[1])
 
 
 def solution(mesh):

time: 400 us -> 268 us (0.67)
  waiting for transfers between devices: 269 us -> 140 us
  between operations: 14.3 us -> 0.88 us
  starting transfers between devices: 28.4 us -> 38 us
    reduce_scatter x2 -> x0, waiting for transfers between devices: 126 us -> none  [the longest x1 75.8 us: local(): lax.psum_scatter(right_term, 'dp', scatter_dimension=1, tiled=True)]
    all_to_all x0 -> x1, starting transfers between devices: none -> 9.99 us  [dp_reduce_scatter(): lax.all_to_all(terms, 'dp', split_axis=2, concat_axis=0, tiled=True)]
    all_to_all x2, waiting for transfers between devices: 72.2 us -> 66.8 us  [local(): lax.all_to_all(permuted_grad, 'block', split_axis=1, concat_axis=0, tiled...]
    unnamed x26 -> x29, local copies, waits for them, and re-layouts: 20.2 us -> 17.5 us
  transfers between devices with their start and end apart: 6 -> 5, of which waited for: 6 -> 5; matrix products, arithmetic and copies ran while one was open for 17% -> 25% of each run, Pallas kernels for 0% -> 0%
where the time goes in v1:
time: 268 us; the launch traced here: 267 us
  waiting for transfers between devices  140 us (52%)
  local copies, waits for them, and re-layouts  45.2 us (17%)
  matrix products  38.1 us (14%)
  starting transfers between devices  38 us (14%)
  other arithmetic  4.58 us (2%)
    all_to_all x2, waiting for transfers between devices, local(): lax.all_to_all(outgoing, 'block', split_axis=0, concat_axis=1, tiled=True)  71.1 us
    all_to_all x2, waiting for transfers between devices, local(): lax.all_to_all(permuted_grad, 'block', split_axis=1, concat_axis=0, tiled...  66.8 us
    unnamed x29, local copies, waits for them, and re-layouts  17.5 us
    all_to_all x2, starting transfers between devices, local(): lax.all_to_all(outgoing, 'block', split_axis=0, concat_axis=1, tiled=True)  15.9 us
    all_to_all x2, starting transfers between devices, local(): lax.all_to_all(permuted_grad, 'block', split_axis=1, concat_axis=0, tiled...  12.1 us
    dot_general x2, matrix products, local(): jnp.einsum('jit,jik->jkt', forward_received, right_factor, preferred_elem...  10.7 us
    all_to_all x1, starting transfers between devices, dp_reduce_scatter(): lax.all_to_all(terms, 'dp', split_axis=2, concat_axis=0, tiled=True)  9.99 us
    convert_element_type x2, local copies, waits for them, and re-layouts, local(): permuted_grad = jnp.einsum('jkt,jik->jit', mixed_grad, right_factor, pref...  8.35 us
  transfers between devices with their start and end apart: 5, of which 5 were waited for; matrix products, arithmetic and copies ran while one was open for 25% of the time, Pallas kernels for 0%

profile of v1, /device:TPU:1, one launch (start us, length us, event | category | flops | bytes accessed | tf_op | source)
XLA Modules:
  0.0 266.7 jit_solution(17563426925048351936)
XLA Ops:
  5.6 10.2 %all-to-all-start.2 = ((bf16[128,8,1024]{2,1,0:T(8,128)(2,1)}), bf16[128,8,1024]{2,1,0:T(8,128)(2,1)S(1)}, u32[]{:S(2)}, u32[]{:S(2)}) async-start(bf16[128,8,1024]{2,1,0:T(8,128)(2,1)} %copy.85), calls=%async_computation.2 | async-start | bytes 4194304 | tf_op jit(solution)/shard_map/all_to_all | solution.py:34
  20.6 43.6 %all-to-all-done.2 = bf16[128,8,1024]{2,1,0:T(8,128)(2,1)S(1)} async-done(((bf16[128,8,1024]{2,1,0:T(8,128)(2,1)}), bf16[128,8,1024]{2,1,0:T(8,128)(2,1)S(1)}, u32[]{:S(2)}, u32[]{:S(2)}) %all-to-all-start.2) | async-done | bytes 2097184 | tf_op jit(solution)/shard_map/all_to_all | solution.py:34
  64.2 5.7 %all-to-all-start = ((bf16[128,8,1024]{2,1,0:T(8,128)(2,1)}), bf16[128,8,1024]{2,1,0:T(8,128)(2,1)}, u32[]{:S(2)}, u32[]{:S(2)}) async-start(bf16[128,8,1024]{2,1,0:T(8,128)(2,1)} %copy.76), calls=%async_computation | async-start | bytes 4194304 | tf_op jit(solution)/shard_map/all_to_all | solution.py:34
  70.0 4.9 %fusion.62 = (bf16[8,128,1024]{2,1,0:T(8,128)(2,1)}, bf16[8,128,1024]{2,1,0:T(8,128)(2,1)}) fusion(bf16[8,128,2048]{2,1,0:T(8,128)(2,1)} %param.7), kind=kLoop, calls=%fused_computation.62 | loop fusion | bytes 8388608 | tf_op jit(solution)/shard_map/slice | solution.py:30
  74.9 3.0 %copy.114 = bf16[8,128,1024]{1,2,0:T(8,128)(2,1)S(1)} copy(bf16[8,128,1024]{2,1,0:T(8,128)(2,1)} %get-tuple-element.16) | data formatting | bytes 4194304
  77.9 5.0 %fusion.2 = bf16[8,128,1024]{1,2,0:T(8,128)(2,1)S(1)} fusion(bf16[8,128,1024]{1,2,0:T(8,128)(2,1)S(1)} %copy.114, bf16[8,128,128]{2,1,0:T(8,128)(2,1)S(1)} %copy-done, bf16[8,16,8,1024]{3,2,0,1:T(8,128)(2,1)} %bitcast.91), kind=kOutput, calls=%fused_computation.10 | convolution fusion | flops 289406976 | bytes 6553600 | tf_op jit(solution)/shard_map/jit,jik->jkt/dot_general | solution.py:37
  86.4 4.2 %copy.88 = bf16[8,128,1024]{2,0,1:T(8,128)(2,1)} copy(bf16[8,128,1024]{1,2,0:T(8,128)(2,1)} %convert_bitcast_fusion) | data formatting | bytes 4194304 | tf_op jit(solution)/shard_map/convert_element_type | solution.py:50
  90.6 27.5 %all-to-all-done = bf16[128,8,1024]{2,1,0:T(8,128)(2,1)} async-done(((bf16[128,8,1024]{2,1,0:T(8,128)(2,1)}), bf16[128,8,1024]{2,1,0:T(8,128)(2,1)}, u32[]{:S(2)}, u32[]{:S(2)}) %all-to-all-start) | async-done | bytes 2097184 | tf_op jit(solution)/shard_map/all_to_all | solution.py:34
  118.1 6.1 %all-to-all-start.3 = ((bf16[8,128,1024]{2,0,1:T(8,128)(2,1)}), bf16[8,128,1024]{2,0,1:T(8,128)(2,1)}, u32[]{:S(2)}, u32[]{:S(2)}) async-start(bf16[8,128,1024]{2,0,1:T(8,128)(2,1)} %copy.88), calls=%async_computation.3 | async-start | bytes 4194304 | tf_op jit(solution)/shard_map/all_to_all | solution.py:51
  124.2 3.9 %copy.113 = bf16[8,128,1024]{1,2,0:T(8,128)(2,1)} copy(bf16[8,128,1024]{2,1,0:T(8,128)(2,1)} %get-tuple-element.15) | data formatting | bytes 4194304
  128.1 5.7 %fusion = bf16[8,128,1024]{1,2,0:T(8,128)(2,1)S(1)} fusion(bf16[8,128,1024]{1,2,0:T(8,128)(2,1)} %copy.113, bf16[8,128,128]{2,1,0:T(8,128)(2,1)S(1)} %copy-done, bf16[8,16,8,1024]{3,2,0,1:T(8,128)(2,1)} %bitcast.2), kind=kOutput, calls=%fused_computation.8 | convolution fusion | flops 289406976 | bytes 6553600 | tf_op jit(solution)/shard_map/jit,jik->jkt/dot_general | solution.py:37
  137.2 4.2 %copy.79 = bf16[8,128,1024]{2,0,1:T(8,128)(2,1)} copy(bf16[8,128,1024]{1,2,0:T(8,128)(2,1)} %convert_bitcast_fusion.2) | data formatting | bytes 4194304 | tf_op jit(solution)/shard_map/convert_element_type | solution.py:50
  141.3 31.0 %all-to-all-done.3 = bf16[8,128,1024]{2,0,1:T(8,128)(2,1)} async-done(((bf16[8,128,1024]{2,0,1:T(8,128)(2,1)}), bf16[8,128,1024]{2,0,1:T(8,128)(2,1)}, u32[]{:S(2)}, u32[]{:S(2)}) %all-to-all-start.3) | async-done | bytes 2097184 | tf_op jit(solution)/shard_map/all_to_all | solution.py:51
  172.4 6.1 %all-to-all-start.1 = ((bf16[8,128,1024]{2,0,1:T(8,128)(2,1)}), bf16[8,128,1024]{2,0,1:T(8,128)(2,1)}, u32[]{:S(2)}, u32[]{:S(2)}) async-start(bf16[8,128,1024]{2,0,1:T(8,128)(2,1)} %copy.79), calls=%async_computation.1 | async-start | bytes 4194304 | tf_op jit(solution)/shard_map/all_to_all | solution.py:51
  178.5 3.2 %fusion.18 = f32[8,128,128]{1,2,0:T(8,128)S(1)} fusion(bf16[8,128,1024]{1,2,0:T(8,128)(2,1)} %copy-done.7, bf16[8,16,8,1024]{3,2,0,1:T(8,128)(2,1)} %bitcast.92), kind=kOutput, calls=%fused_computation.29 | convolution fusion | flops 268435456 | bytes 4718592 | tf_op jit(solution)/shard_map/jit,jkt->jik/dot_general | solution.py:43
  181.6 2.5 fusion.44
  184.1 3.2 %copy.90 = bf16[16,8,8,1024]{3,2,1,0:T(8,128)(2,1)S(1)} copy(bf16[16,8,8,1024]{3,1,2,0:T(8,128)(2,1)} %bitcast.19) | data formatting | bytes 4194304 | tf_op jit(solution)/shard_map/all_to_all | solution.py:51
  190.9 35.7 %all-to-all-done.1 = bf16[8,128,1024]{2,0,1:T(8,128)(2,1)} async-done(((bf16[8,128,1024]{2,0,1:T(8,128)(2,1)}), bf16[8,128,1024]{2,0,1:T(8,128)(2,1)}, u32[]{:S(2)}, u32[]{:S(2)}) %all-to-all-start.1) | async-done | bytes 2097184 | tf_op jit(solution)/shard_map/all_to_all | solution.py:51
  226.6 3.2 %copy.81 = bf16[16,8,8,1024]{3,2,1,0:T(8,128)(2,1)S(1)} copy(bf16[16,8,8,1024]{3,1,2,0:T(8,128)(2,1)} %bitcast.8) | data formatting | bytes 4194304 | tf_op jit(solution)/shard_map/all_to_all | solution.py:51
  229.8 4.1 %fusion.57 = f32[1,8,128,128]{2,3,1,0:T(8,128)S(1)} fusion(f32[8,128,128]{2,1,0:T(8,128)} %fusion.25, bf16[8,128,2048]{2,1,0:T(8,128)(2,1)S(1)} %copy-done.12, bf16[128,8,1024]{2,1,0:T(8,128)(2,1)S(1)} %bitcast.89), kind=kOutput, calls=%fused_computation.58 | convolution fusion | flops 268697600 | bytes 5242880 | tf_op jit(solution)/shard_map/ict,oit->ico/dot_general | solution.py:58
  235.0 2.6 copy.99
  237.6 10.0 %all-to-all-start.4 = ((f32[2,8,128,128]{3,1,0,2:T(8,128)}), f32[2,8,128,128]{3,1,0,2:T(8,128)}, u32[]{:S(2)}, u32[]{:S(2)}) async-start(f32[2,8,128,128]{3,1,0,2:T(8,128)} %copy.99), calls=%async_computation.4 | async-start | bytes 2097152 | tf_op jit(solution)/shard_map/all_to_all | solution.py:15
  247.6 4.1 %fusion.3 = bf16[8,128,1024]{1,2,0:T(8,128)(2,1)S(1)} fusion(bf16[8,128,1024]{1,2,0:T(8,128)(2,1)S(1)} %copy.114, bf16[8,128,128]{2,1,0:T(8,128)(2,1)S(1)} %copy-done.10, bf16[128,8,1024]{2,1,0:T(8,128)(2,1)} %bitcast.88), kind=kOutput, calls=%fused_computation.11 | convolution fusion | flops 271581184 | bytes 6553600 | tf_op jit(solution)/shard_map/oit,ico->ict/dot_general | solution.py:52
  256.3 6.5 %copy.101 = bf16[8,128,2048]{2,1,0:T(8,128)(2,1)} copy(bf16[8,128,2048]{1,2,0:T(8,128)(2,1)} %pad_maximum_fusion) | data formatting | bytes 8388608
  (40 shorter events, 29.8 us)
Async XLA Ops:
  0.6 77.3 %copy-start = (bf16[8,128,128]{2,1,0:T(8,128)(2,1)S(1)}, bf16[8,128,128]{2,1,0:T(8,128)(2,1)}, u32[]{:S(2)}) copy-start(bf16[8,128,128]{2,1,0:T(8,128)(2,1)} %param.6) | copy-start | bytes 786436
  5.6 10.2 %copy-start.10 = (bf16[8,128,128]{2,1,0:T(8,128)(2,1)S(1)}, bf16[8,128,128]{2,1,0:T(8,128)(2,1)}, u32[]{:S(2)}) copy-start(bf16[8,128,128]{2,1,0:T(8,128)(2,1)} %param.5) | copy-start | bytes 786436
  5.6 58.6 %all-to-all-start.2 = ((bf16[128,8,1024]{2,1,0:T(8,128)(2,1)}), bf16[128,8,1024]{2,1,0:T(8,128)(2,1)S(1)}, u32[]{:S(2)}, u32[]{:S(2)}) async-start(bf16[128,8,1024]{2,1,0:T(8,128)(2,1)} %copy.85), calls=%async_computation.2 | async-start | bytes 4194304 | tf_op jit(solution)/shard_map/all_to_all | solution.py:34
  64.2 10.6 %copy-start.6 = (bf16[128,8,1024]{2,1,0:T(8,128)(2,1)}, bf16[128,8,1024]{2,1,0:T(8,128)(2,1)S(1)}, u32[]{:S(2)}) copy-start(bf16[128,8,1024]{2,1,0:T(8,128)(2,1)S(1)} %all-to-all-done.2) | copy-start | bytes 6291460
  64.2 53.9 %all-to-all-start = ((bf16[128,8,1024]{2,1,0:T(8,128)(2,1)}), bf16[128,8,1024]{2,1,0:T(8,128)(2,1)}, u32[]{:S(2)}, u32[]{:S(2)}) async-start(bf16[128,8,1024]{2,1,0:T(8,128)(2,1)} %copy.76), calls=%async_computation | async-start | bytes 4194304 | tf_op jit(solution)/shard_map/all_to_all | solution.py:34
  82.9 1.4 copy-start.7
  118.1 54.2 %all-to-all-start.3 = ((bf16[8,128,1024]{2,0,1:T(8,128)(2,1)}), bf16[8,128,1024]{2,0,1:T(8,128)(2,1)}, u32[]{:S(2)}, u32[]{:S(2)}) async-start(bf16[8,128,1024]{2,0,1:T(8,128)(2,1)} %copy.88), calls=%async_computation.3 | async-start | bytes 4194304 | tf_op jit(solution)/shard_map/all_to_all | solution.py:51
  133.8 1.3 copy-start.8
  172.4 54.2 %all-to-all-start.1 = ((bf16[8,128,1024]{2,0,1:T(8,128)(2,1)}), bf16[8,128,1024]{2,0,1:T(8,128)(2,1)}, u32[]{:S(2)}, u32[]{:S(2)}) async-start(bf16[8,128,1024]{2,0,1:T(8,128)(2,1)} %copy.79), calls=%async_computation.1 | async-start | bytes 4194304 | tf_op jit(solution)/shard_map/all_to_all | solution.py:51
  178.4 3.2 %copy-start.9 = (bf16[8,128,1024]{1,2,0:T(8,128)(2,1)S(1)}, bf16[8,128,1024]{1,2,0:T(8,128)(2,1)}, u32[]{:S(2)}) copy-start(bf16[8,128,1024]{1,2,0:T(8,128)(2,1)} %copy-done.8) | copy-start | bytes 6291460
  184.1 4.5 %copy-start.11 = (bf16[8,128,2048]{2,1,0:T(8,128)(2,1)S(1)}, bf16[8,128,2048]{2,1,0:T(8,128)(2,1)}, u32[]{:S(2)}) copy-start(bf16[8,128,2048]{2,1,0:T(8,128)(2,1)} %param.4) | copy-start | bytes 12582916
  187.3 1.3 copy-start.3
  226.6 3.2 %copy-start.12 = (bf16[8,128,2048]{2,1,0:T(8,128)(2,1)S(1)}, bf16[8,128,2048]{2,1,0:T(8,128)(2,1)}, u32[]{:S(2)}) copy-start(bf16[8,128,2048]{2,1,0:T(8,128)(2,1)} %param.4) | copy-start | bytes 12582916
  229.8 4.1 %copy-start.4 = (bf16[16,8,8,1024]{3,2,1,0:T(8,128)(2,1)}, bf16[16,8,8,1024]{3,2,1,0:T(8,128)(2,1)S(1)}, u32[]{:S(2)}) copy-start(bf16[16,8,8,1024]{3,2,1,0:T(8,128)(2,1)S(1)} %copy.81) | copy-start | bytes 6291460
  237.6 27.2 %all-to-all-start.4 = ((f32[2,8,128,128]{3,1,0,2:T(8,128)}), f32[2,8,128,128]{3,1,0,2:T(8,128)}, u32[]{:S(2)}, u32[]{:S(2)}) async-start(f32[2,8,128,128]{3,1,0,2:T(8,128)} %copy.99), calls=%async_computation.4 | async-start | bytes 2097152 | tf_op jit(solution)/shard_map/all_to_all | solution.py:15
  247.6 4.2 %copy-start.2 = (bf16[8,128,1024]{1,2,0:T(8,128)(2,1)S(1)}, bf16[8,128,1024]{1,2,0:T(8,128)(2,1)}, u32[]{:S(2)}) copy-start(bf16[8,128,1024]{1,2,0:T(8,128)(2,1)} %copy.113) | copy-start | bytes 6291460
  247.6 4.2 %copy-start.5 = (bf16[16,8,8,1024]{3,2,1,0:T(8,128)(2,1)S(1)}, bf16[16,8,8,1024]{3,2,1,0:T(8,128)(2,1)}, u32[]{:S(2)}) copy-start(bf16[16,8,8,1024]{3,2,1,0:T(8,128)(2,1)} %copy-done.4) | copy-start | bytes 6291460
  256.3 10.4 %copy-start.1 = (bf16[8,128,128]{2,1,0:T(8,128)(2,1)S(1)}, bf16[8,128,128]{2,1,0:T(8,128)(2,1)}, u32[]{:S(2)}) copy-start(bf16[8,128,128]{2,1,0:T(8,128)(2,1)} %param.6) | copy-start | bytes 786436

commit v2 on v1

--- a/solution.py
+++ b/solution.py
@@ -3,7 +3,8 @@
 from jax import lax
 from jax.sharding import PartitionSpec as P
 
-MICRO = 2
+CHUNKS = (3, 1)
+SPLIT_DP = False
 
 
 def gelu_slope(values):
@@ -20,14 +21,18 @@
 def local(inputs, left_factor, right_factor, cotangent):
     tokens_local = inputs.shape[2]
     scale = float(lax.axis_size("dp") * tokens_local) ** (-0.5)
-    groups = MICRO
-    group_width = tokens_local // groups
+    total = sum(CHUNKS)
+    bounds = [0]
+    for share in CHUNKS:
+        bounds.append(bounds[-1] + tokens_local * share // total)
     input_pieces = []
     grad_left = None
     grad_right = None
-    for group in range(groups):
-        x_group = inputs[:, :, group * group_width : (group + 1) * group_width]
-        dy_group = cotangent[:, :, group * group_width : (group + 1) * group_width]
+    right_done = None
+    for group in range(len(CHUNKS)):
+        lo, hi = bounds[group], bounds[group + 1]
+        x_group = inputs[:, :, lo:hi]
+        dy_group = cotangent[:, :, lo:hi]
         outgoing = jnp.einsum(
             "ict,ico->oit", x_group, left_factor, preferred_element_type=jnp.float32
         ).astype(jnp.bfloat16)
@@ -45,6 +50,9 @@
             )
             * scale
         )
+        grad_right = right_term if grad_right is None else grad_right + right_term
+        if SPLIT_DP and group == len(CHUNKS) - 1:
+            right_done = dp_reduce_scatter(grad_right[None])[0]
         permuted_grad = jnp.einsum(
             "jkt,jik->jit", mixed_grad, right_factor, preferred_element_type=jnp.float32
         ).astype(jnp.bfloat16)
@@ -59,8 +67,9 @@
             * scale
         )
         grad_left = left_term if grad_left is None else grad_left + left_term
-        grad_right = right_term if grad_right is None else grad_right + right_term
     input_grad = jnp.concatenate(input_pieces, axis=2)
+    if SPLIT_DP:
+        return (input_grad, dp_reduce_scatter(grad_left[None])[0], right_done)
     reduced = dp_reduce_scatter(jnp.stack([grad_left, grad_right]))
     return (input_grad, reduced[0], reduced[1])
 

time: 268 us -> 262 us (0.978)
  waiting for transfers between devices: 140 us -> 158 us
  local copies, waits for them, and re-layouts: 45.2 us -> 31.9 us
  matrix products: 38.1 us -> 29 us
    all_to_all x2, waiting for transfers between devices: 71.1 us -> 85.6 us  [local(): lax.all_to_all(outgoing, 'block', split_axis=0, concat_axis=1, tiled=True)]
    dot_general x2, matrix products: 6.36 us -> 2.17 us  [local(): jnp.einsum('ict,oit->ico', x_group, received, preferred_element_type=jnp....]
    all_to_all x2, waiting for transfers between devices: 66.8 us -> 70.8 us  [local(): lax.all_to_all(permuted_grad, 'block', split_axis=1, concat_axis=0, tiled...]
    unnamed x29 -> x33, local copies, waits for them, and re-layouts: 17.5 us -> 14.1 us
    convert_element_type x2, local copies, waits for them, and re-layouts: 8.35 us -> 5.15 us  [local(): permuted_grad = jnp.einsum('jkt,jik->jit', mixed_grad, right_factor, pref...]
    slice x1 -> x4, local copies, waits for them, and re-layouts: 4.89 us -> 1.89 us  [local(): dy_group = cotangent[:, :, lo:hi]]
    dot_general x2, matrix products: 4.13 us -> 1.41 us  [local(): jnp.einsum('jkt,jik->jit', mixed_grad, right_factor, preferred_element_ty...]
  transfers between devices with their start and end apart: 5 -> 5, of which waited for: 5 -> 5; matrix products, arithmetic and copies ran while one was open for 25% -> 18% of each run, Pallas kernels for 0% -> 0%
where the time goes in v2:
time: 262 us; the launch traced here: 261 us
  waiting for transfers between devices  158 us (60%)
  starting transfers between devices  36.9 us (14%)
  local copies, waits for them, and re-layouts  31.9 us (12%)
  matrix products  29 us (11%)
  other arithmetic  3.59 us (1%)
    all_to_all x2, waiting for transfers between devices, local(): lax.all_to_all(outgoing, 'block', split_axis=0, concat_axis=1, tiled=True)  85.6 us
    all_to_all x2, waiting for transfers between devices, local(): lax.all_to_all(permuted_grad, 'block', split_axis=1, concat_axis=0, tiled...  70.8 us
    all_to_all x2, starting transfers between devices, local(): lax.all_to_all(outgoing, 'block', split_axis=0, concat_axis=1, tiled=True)  16.3 us
    unnamed x33, local copies, waits for them, and re-layouts  14.1 us
    all_to_all x2, starting transfers between devices, local(): lax.all_to_all(permuted_grad, 'block', split_axis=1, concat_axis=0, tiled...  11.7 us
    all_to_all x1, starting transfers between devices, dp_reduce_scatter(): lax.all_to_all(terms, 'dp', split_axis=2, concat_axis=0, tiled=True)  8.82 us
    dot_general x2, matrix products, local(): jnp.einsum('jit,jik->jkt', forward_received, right_factor, preferred_elem...  8.81 us
    dot_general x2, matrix products, local(): jnp.einsum('oit,ico->ict', received, left_factor, preferred_element_type=...  6.43 us
  transfers between devices with their start and end apart: 5, of which 5 were waited for; matrix products, arithmetic and copies ran while one was open for 18% of the time, Pallas kernels for 0%

profile of v2, /device:TPU:1, one launch (start us, length us, event | category | flops | bytes accessed | tf_op | source)
XLA Modules:
  0.0 260.7 jit_solution(140615023599947295)
XLA Ops:
  0.7 1.8 fusion.30
  4.1 10.0 %all-to-all-start.2 = ((bf16[128,8,512]{2,1,0:T(8,128)(2,1)}), bf16[128,8,512]{2,1,0:T(8,128)(2,1)S(1)}, u32[]{:S(2)}, u32[]{:S(2)}) async-start(bf16[128,8,512]{2,1,0:T(8,128)(2,1)} %copy.85), calls=%async_computation.2 | async-start | bytes 2097152 | tf_op jit(solution)/shard_map/all_to_all | solution.py:39
  14.2 2.9 %fusion.9 = bf16[128,8,1536]{2,0,1:T(8,128)(2,1)S(1)} fusion(bf16[8,128,128]{2,1,0:T(8,128)(2,1)S(1)} %copy-done.11, bf16[8,128,2048]{2,1,0:T(8,128)(2,1)} %param.4), kind=kOutput, calls=%fused_computation.17 | convolution fusion | flops 404226048 | bytes 6553600 | tf_op jit(solution)/shard_map/ict,ico->oit/dot_general | solution.py:36
  17.1 3.4 %copy.76 = bf16[128,8,1536]{2,1,0:T(8,128)(2,1)} copy(bf16[128,8,1536]{2,0,1:T(8,128)(2,1)S(1)} %fusion.9) | data formatting | bytes 6291456 | tf_op jit(solution)/shard_map/convert_element_type | solution.py:38
  20.5 19.1 %all-to-all-done.2 = bf16[128,8,512]{2,1,0:T(8,128)(2,1)S(1)} async-done(((bf16[128,8,512]{2,1,0:T(8,128)(2,1)}), bf16[128,8,512]{2,1,0:T(8,128)(2,1)S(1)}, u32[]{:S(2)}, u32[]{:S(2)}) %all-to-all-start.2) | async-done | bytes 1048608 | tf_op jit(solution)/shard_map/all_to_all | solution.py:39
  39.6 6.3 %all-to-all-start = ((bf16[128,8,1536]{2,1,0:T(8,128)(2,1)}), bf16[128,8,1536]{2,1,0:T(8,128)(2,1)}, u32[]{:S(2)}, u32[]{:S(2)}) async-start(bf16[128,8,1536]{2,1,0:T(8,128)(2,1)} %copy.76), calls=%async_computation | async-start | bytes 6291456 | tf_op jit(solution)/shard_map/all_to_all | solution.py:39
  46.6 1.7 fusion.21
  51.5 66.5 %all-to-all-done = bf16[128,8,1536]{2,1,0:T(8,128)(2,1)} async-done(((bf16[128,8,1536]{2,1,0:T(8,128)(2,1)}), bf16[128,8,1536]{2,1,0:T(8,128)(2,1)}, u32[]{:S(2)}, u32[]{:S(2)}) %all-to-all-start) | async-done | bytes 3145760 | tf_op jit(solution)/shard_map/all_to_all | solution.py:39
  117.9 4.6 %all-to-all-start.3 = ((bf16[8,128,512]{2,0,1:T(8,128)(2,1)}), bf16[8,128,512]{2,0,1:T(8,128)(2,1)}, u32[]{:S(2)}, u32[]{:S(2)}) async-start(bf16[8,128,512]{2,0,1:T(8,128)(2,1)} %copy.88), calls=%async_computation.3 | async-start | bytes 2097152 | tf_op jit(solution)/shard_map/all_to_all | solution.py:59
  122.6 1.9 slice-done.1
  124.5 2.8 %copy.113 = bf16[8,128,1536]{1,2,0:T(8,128)(2,1)} copy(bf16[8,128,1536]{2,1,0:T(8,128)(2,1)S(1)} %slice-done.1) | data formatting | bytes 6291456
  127.2 7.1 %fusion = bf16[8,128,1536]{1,2,0:T(8,128)(2,1)S(1)} fusion(bf16[8,128,1536]{1,2,0:T(8,128)(2,1)} %copy.113, bf16[8,128,128]{2,1,0:T(8,128)(2,1)S(1)} %copy-done, bf16[8,16,8,1536]{3,2,0,1:T(8,128)(2,1)} %bitcast.2), kind=kOutput, calls=%fused_computation.4 | convolution fusion | flops 434110464 | bytes 9699328 | tf_op jit(solution)/shard_map/jit,jik->jkt/dot_general | solution.py:42
  137.0 3.4 %copy.79 = bf16[8,128,1536]{2,0,1:T(8,128)(2,1)} copy(bf16[8,128,1536]{1,2,0:T(8,128)(2,1)S(1)} %fusion.10) | data formatting | bytes 6291456 | tf_op jit(solution)/shard_map/convert_element_type | solution.py:58
  140.5 6.7 %all-to-all-done.3 = bf16[8,128,512]{2,0,1:T(8,128)(2,1)} async-done(((bf16[8,128,512]{2,0,1:T(8,128)(2,1)}), bf16[8,128,512]{2,0,1:T(8,128)(2,1)}, u32[]{:S(2)}, u32[]{:S(2)}) %all-to-all-start.3) | async-done | bytes 1048608 | tf_op jit(solution)/shard_map/all_to_all | solution.py:59
  147.2 7.1 %all-to-all-start.1 = ((bf16[8,128,1536]{2,0,1:T(8,128)(2,1)}), bf16[8,128,1536]{2,0,1:T(8,128)(2,1)S(1)}, u32[]{:S(2)}, u32[]{:S(2)}) async-start(bf16[8,128,1536]{2,0,1:T(8,128)(2,1)} %copy.79), calls=%async_computation.1 | async-start | bytes 6291456 | tf_op jit(solution)/shard_map/all_to_all | solution.py:59
  154.3 2.6 copy.90
  156.9 4.1 %fusion.11 = f32[8,128,128]{1,2,0:T(8,128)S(1)} fusion(bf16[8,128,1536]{1,2,0:T(8,128)(2,1)} %copy-done.13, bf16[8,16,8,1536]{3,2,0,1:T(8,128)(2,1)} %bitcast.2), kind=kOutput, calls=%fused_computation.19 | convolution fusion | flops 402653184 | bytes 6815744 | tf_op jit(solution)/shard_map/jit,jkt->jik/dot_general | solution.py:48
  162.3 64.1 %all-to-all-done.1 = bf16[8,128,1536]{2,0,1:T(8,128)(2,1)S(1)} async-done(((bf16[8,128,1536]{2,0,1:T(8,128)(2,1)}), bf16[8,128,1536]{2,0,1:T(8,128)(2,1)S(1)}, u32[]{:S(2)}, u32[]{:S(2)}) %all-to-all-start.1) | async-done | bytes 3145760 | tf_op jit(solution)/shard_map/all_to_all | solution.py:59
  232.7 8.8 %all-to-all-start.4 = ((f32[2,8,128,128]{3,1,0,2:T(8,128)}), f32[2,8,128,128]{3,1,0,2:T(8,128)}, u32[]{:S(2)}, u32[]{:S(2)}) async-start(f32[2,8,128,128]{3,1,0,2:T(8,128)} %copy.99), calls=%async_computation.4 | async-start | bytes 2097152 | tf_op jit(solution)/shard_map/all_to_all | solution.py:16
  241.5 2.2 fusion.22
  243.8 4.2 %fusion.1 = bf16[8,128,1536]{1,2,0:T(8,128)(2,1)S(1)} fusion(bf16[8,128,1536]{1,2,0:T(8,128)(2,1)S(1)} %copy-done.2, bf16[8,128,128]{2,1,0:T(8,128)(2,1)S(1)} %copy-done.12, bf16[128,8,1536]{2,1,0:T(8,128)(2,1)} %bitcast.83), kind=kOutput, calls=%fused_computation.5 | convolution fusion | flops 407371776 | bytes 9699328 | tf_op jit(solution)/shard_map/oit,ico->ict/dot_general | solution.py:60
  248.0 2.2 pad_maximum_fusion
  250.2 6.4 %copy.101 = bf16[8,128,2048]{2,1,0:T(8,128)(2,1)} copy(bf16[8,128,2048]{1,2,0:T(8,128)(2,1)} %pad_maximum_fusion) | data formatting | bytes 8388608
  256.7 2.0 all-to-all-done.4
  (47 shorter events, 17.6 us)
Async XLA Ops:
  0.6 45.9 %copy-start = (bf16[8,128,128]{2,1,0:T(8,128)(2,1)S(1)}, bf16[8,128,128]{2,1,0:T(8,128)(2,1)}, u32[]{:S(2)}) copy-start(bf16[8,128,128]{2,1,0:T(8,128)(2,1)} %param.6) | copy-start | bytes 786436
  0.6 13.5 %copy-start.11 = (bf16[8,128,128]{2,1,0:T(8,128)(2,1)S(1)}, bf16[8,128,128]{2,1,0:T(8,128)(2,1)}, u32[]{:S(2)}) copy-start(bf16[8,128,128]{2,1,0:T(8,128)(2,1)} %param.5) | copy-start | bytes 786436
  4.1 35.5 %all-to-all-start.2 = ((bf16[128,8,512]{2,1,0:T(8,128)(2,1)}), bf16[128,8,512]{2,1,0:T(8,128)(2,1)S(1)}, u32[]{:S(2)}, u32[]{:S(2)}) async-start(bf16[128,8,512]{2,1,0:T(8,128)(2,1)} %copy.85), calls=%async_computation.2 | async-start | bytes 2097152 | tf_op jit(solution)/shard_map/all_to_all | solution.py:39
  20.5 25.4 %slice-start = ((bf16[8,128,2048]{2,1,0:T(8,128)(2,1)}), bf16[8,128,512]{2,1,0:T(8,128)(2,1)S(1)}, s32[]{:S(2)}) async-start(bf16[8,128,2048]{2,1,0:T(8,128)(2,1)} %param.7), calls=%async_computation.5 | async-start | bytes 2097152 | tf_op jit(solution)/shard_map/slice | solution.py:35
  39.6 7.0 %copy-start.4 = (bf16[128,8,512]{2,1,0:T(8,128)(2,1)}, bf16[128,8,512]{2,1,0:T(8,128)(2,1)S(1)}, u32[]{:S(2)}) copy-start(bf16[128,8,512]{2,1,0:T(8,128)(2,1)S(1)} %all-to-all-done.2) | copy-start | bytes 3145732
  39.6 78.4 %all-to-all-start = ((bf16[128,8,1536]{2,1,0:T(8,128)(2,1)}), bf16[128,8,1536]{2,1,0:T(8,128)(2,1)}, u32[]{:S(2)}, u32[]{:S(2)}) async-start(bf16[128,8,1536]{2,1,0:T(8,128)(2,1)} %copy.76), calls=%async_computation | async-start | bytes 6291456 | tf_op jit(solution)/shard_map/all_to_all | solution.py:39
  46.5 1.8 copy-start.9
  48.3 1.0 copy-start.6
  117.9 29.2 %all-to-all-start.3 = ((bf16[8,128,512]{2,0,1:T(8,128)(2,1)}), bf16[8,128,512]{2,0,1:T(8,128)(2,1)}, u32[]{:S(2)}, u32[]{:S(2)}) async-start(bf16[8,128,512]{2,0,1:T(8,128)(2,1)} %copy.88), calls=%async_computation.3 | async-start | bytes 2097152 | tf_op jit(solution)/shard_map/all_to_all | solution.py:59
  122.6 1.9 slice-start.1
  134.3 1.7 copy-start.13
  147.2 79.3 %all-to-all-start.1 = ((bf16[8,128,1536]{2,0,1:T(8,128)(2,1)}), bf16[8,128,1536]{2,0,1:T(8,128)(2,1)S(1)}, u32[]{:S(2)}, u32[]{:S(2)}) async-start(bf16[8,128,1536]{2,0,1:T(8,128)(2,1)} %copy.79), calls=%async_computation.1 | async-start | bytes 6291456 | tf_op jit(solution)/shard_map/all_to_all | solution.py:59
  156.9 4.1 %copy-start.5 = (bf16[128,8,512]{2,1,0:T(8,128)(2,1)S(1)}, bf16[128,8,512]{2,1,0:T(8,128)(2,1)}, u32[]{:S(2)}) copy-start(bf16[128,8,512]{2,1,0:T(8,128)(2,1)} %copy-done.4) | copy-start | bytes 3145732
  156.9 4.1 %copy-start.7 = (bf16[8,128,512]{1,2,0:T(8,128)(2,1)S(1)}, bf16[8,128,512]{1,2,0:T(8,128)(2,1)}, u32[]{:S(2)}) copy-start(bf16[8,128,512]{1,2,0:T(8,128)(2,1)} %copy-done.6) | copy-start | bytes 3145732
  226.4 2.4 copy-start.8
  227.6 2.6 copy-start.3
  228.8 1.4 copy-start.10
  230.2 1.0 copy-start.14
  231.2 10.3 %copy-start.12 = (bf16[8,128,128]{2,1,0:T(8,128)(2,1)S(1)}, bf16[8,128,128]{2,1,0:T(8,128)(2,1)}, u32[]{:S(2)}) copy-start(bf16[8,128,128]{2,1,0:T(8,128)(2,1)} %param.5) | copy-start | bytes 786436
  232.7 11.1 %copy-start.2 = (bf16[8,128,1536]{1,2,0:T(8,128)(2,1)S(1)}, bf16[8,128,1536]{1,2,0:T(8,128)(2,1)}, u32[]{:S(2)}) copy-start(bf16[8,128,1536]{1,2,0:T(8,128)(2,1)} %copy.113) | copy-start | bytes 9437188
  232.7 26.0 %all-to-all-start.4 = ((f32[2,8,128,128]{3,1,0,2:T(8,128)}), f32[2,8,128,128]{3,1,0,2:T(8,128)}, u32[]{:S(2)}, u32[]{:S(2)}) async-start(f32[2,8,128,128]{3,1,0,2:T(8,128)} %copy.99), calls=%async_computation.4 | async-start | bytes 2097152 | tf_op jit(solution)/shard_map/all_to_all | solution.py:16
  248.0 12.7 %copy-start.1 = (bf16[8,128,128]{2,1,0:T(8,128)(2,1)S(1)}, bf16[8,128,128]{2,1,0:T(8,128)(2,1)}, u32[]{:S(2)}) copy-start(bf16[8,128,128]{2,1,0:T(8,128)(2,1)} %param.6) | copy-start | bytes 786436

commit v3 on v2

--- a/solution.py
+++ b/solution.py
@@ -3,7 +3,7 @@
 from jax import lax
 from jax.sharding import PartitionSpec as P
 
-CHUNKS = (3, 1)
+CHUNKS = (13, 3)
 SPLIT_DP = False
 
 

time: 262 us -> 261 us (level)
  local copies, waits for them, and re-layouts: 31.9 us -> 37 us
  starting transfers between devices: 36.9 us -> 33.5 us
    all_to_all x2, waiting for transfers between devices: 85.6 us -> 78.8 us  [local(): lax.all_to_all(outgoing, 'block', split_axis=0, concat_axis=1, tiled=True)]
    all_to_all x2, waiting for transfers between devices: 70.8 us -> 74.9 us  [local(): lax.all_to_all(permuted_grad, 'block', split_axis=1, concat_axis=0, tiled...]
    unnamed x33 -> x27, local copies, waits for them, and re-layouts: 14.1 us -> 15.9 us
  transfers between devices with their start and end apart: 5 -> 5, of which waited for: 5 -> 5; matrix products, arithmetic and copies ran while one was open for 18% -> 22% of each run, Pallas kernels for 0% -> 0%
where the time goes in v3:
time: 261 us; the launch traced here: 260 us
  waiting for transfers between devices  157 us (60%)
  local copies, waits for them, and re-layouts  37 us (14%)
  starting transfers between devices  33.5 us (13%)
  matrix products  29.2 us (11%)
    all_to_all x2, waiting for transfers between devices, local(): lax.all_to_all(outgoing, 'block', split_axis=0, concat_axis=1, tiled=True)  78.8 us
    all_to_all x2, waiting for transfers between devices, local(): lax.all_to_all(permuted_grad, 'block', split_axis=1, concat_axis=0, tiled...  74.9 us
    unnamed x27, local copies, waits for them, and re-layouts  15.9 us
    all_to_all x2, starting transfers between devices, local(): lax.all_to_all(outgoing, 'block', split_axis=0, concat_axis=1, tiled=True)  15.4 us
    all_to_all x2, starting transfers between devices, local(): lax.all_to_all(permuted_grad, 'block', split_axis=1, concat_axis=0, tiled...  9.67 us
    dot_general x2, matrix products, local(): jnp.einsum('jit,jik->jkt', forward_received, right_factor, preferred_elem...  8.9 us
    all_to_all x1, starting transfers between devices, dp_reduce_scatter(): lax.all_to_all(terms, 'dp', split_axis=2, concat_axis=0, tiled=True)  8.45 us
    convert_element_type x2, local copies, waits for them, and re-layouts, local(): permuted_grad = jnp.einsum('jkt,jik->jit', mixed_grad, right_factor, pref...  7.3 us
  transfers between devices with their start and end apart: 5, of which 5 were waited for; matrix products, arithmetic and copies ran while one was open for 22% of the time, Pallas kernels for 0%

profile of v3, /device:TPU:1, one launch (start us, length us, event | category | flops | bytes accessed | tf_op | source)
XLA Modules:
  0.0 259.9 jit_solution(1413870222509505531)
XLA Ops:
  0.7 1.7 fusion.30
  3.7 10.0 %all-to-all-start.2 = ((bf16[128,8,384]{2,1,0:T(8,128)(2,1)}), bf16[128,8,384]{2,1,0:T(8,128)(2,1)S(1)}, u32[]{:S(2)}, u32[]{:S(2)}) async-start(bf16[128,8,384]{2,1,0:T(8,128)(2,1)} %copy.85), calls=%async_computation.2 | async-start | bytes 1572864 | tf_op jit(solution)/shard_map/all_to_all | solution.py:39
  13.7 3.1 %fusion.12 = bf16[128,8,1664]{2,0,1:T(8,128)(2,1)S(1)} fusion(bf16[8,128,128]{2,1,0:T(8,128)(2,1)S(1)} %copy-done.4, bf16[8,128,2048]{2,1,0:T(8,128)(2,1)} %param.4), kind=kOutput, calls=%fused_computation.20 | convolution fusion | flops 437911552 | bytes 7077888 | tf_op jit(solution)/shard_map/ict,ico->oit/dot_general | solution.py:36
  16.8 3.7 %copy.76 = bf16[128,8,1664]{2,1,0:T(8,128)(2,1)} copy(bf16[128,8,1664]{2,0,1:T(8,128)(2,1)S(1)} %fusion.12) | data formatting | bytes 6815744 | tf_op jit(solution)/shard_map/convert_element_type | solution.py:38
  20.5 14.0 %all-to-all-done.2 = bf16[128,8,384]{2,1,0:T(8,128)(2,1)S(1)} async-done(((bf16[128,8,384]{2,1,0:T(8,128)(2,1)}), bf16[128,8,384]{2,1,0:T(8,128)(2,1)S(1)}, u32[]{:S(2)}, u32[]{:S(2)}) %all-to-all-start.2) | async-done | bytes 786464 | tf_op jit(solution)/shard_map/all_to_all | solution.py:39
  35.4 5.3 %all-to-all-start = ((bf16[128,8,1664]{2,1,0:T(8,128)(2,1)}), bf16[128,8,1664]{2,1,0:T(8,128)(2,1)}, u32[]{:S(2)}, u32[]{:S(2)}) async-start(bf16[128,8,1664]{2,1,0:T(8,128)(2,1)} %copy.76), calls=%async_computation | async-start | bytes 6815744 | tf_op jit(solution)/shard_map/all_to_all | solution.py:39
  40.7 4.1 %slice.18 = bf16[8,128,1664]{2,1,0:T(8,128)(2,1)} slice(bf16[8,128,2048]{2,1,0:T(8,128)(2,1)} %param.7), slice={[0:8], [0:128], [0:1664]} | slice | bytes 6815744 | tf_op jit(solution)/shard_map/slice | solution.py:35
  45.2 5.9 %copy.113 = bf16[8,128,1664]{1,2,0:T(8,128)(2,1)} copy(bf16[8,128,1664]{2,1,0:T(8,128)(2,1)} %slice.18) | data formatting | bytes 6815744
  54.1 64.7 %all-to-all-done = bf16[128,8,1664]{2,1,0:T(8,128)(2,1)} async-done(((bf16[128,8,1664]{2,1,0:T(8,128)(2,1)}), bf16[128,8,1664]{2,1,0:T(8,128)(2,1)}, u32[]{:S(2)}, u32[]{:S(2)}) %all-to-all-start) | async-done | bytes 3407904 | tf_op jit(solution)/shard_map/all_to_all | solution.py:39
  118.9 4.1 %all-to-all-start.3 = ((bf16[8,128,384]{2,0,1:T(8,128)(2,1)}), bf16[8,128,384]{2,0,1:T(8,128)(2,1)S(1)}, u32[]{:S(2)}, u32[]{:S(2)}) async-start(bf16[8,128,384]{2,0,1:T(8,128)(2,1)} %copy.88), calls=%async_computation.3 | async-start | bytes 1572864 | tf_op jit(solution)/shard_map/all_to_all | solution.py:59
  123.0 7.6 %fusion = bf16[8,128,1664]{1,2,0:T(8,128)(2,1)S(1)} fusion(bf16[8,128,1664]{1,2,0:T(8,128)(2,1)} %copy.113, bf16[8,128,128]{2,1,0:T(8,128)(2,1)S(1)} %copy-done, bf16[8,16,8,1664]{3,2,0,1:T(8,128)(2,1)} %bitcast.2), kind=kOutput, calls=%fused_computation.4 | convolution fusion | flops 470286336 | bytes 10485760 | tf_op jit(solution)/shard_map/jit,jik->jkt/dot_general | solution.py:42
  130.6 1.7 copy-done.5
  132.3 2.8 %fusion.13 = bf16[8,128,1664]{1,2,0:T(8,128)(2,1)} fusion(bf16[8,128,1664]{1,2,0:T(8,128)(2,1)S(1)} %fusion, bf16[8,128,128]{2,1,0:T(8,128)(2,1)S(1)} %copy-done), kind=kOutput, calls=%fused_computation.21 | convolution fusion | flops 437911552 | bytes 7077888 | tf_op jit(solution)/shard_map/jkt,jik->jit/dot_general | solution.py:56
  135.1 6.0 %copy.79 = bf16[8,128,1664]{2,0,1:T(8,128)(2,1)} copy(bf16[8,128,1664]{1,2,0:T(8,128)(2,1)} %fusion.13) | data formatting | bytes 6815744 | tf_op jit(solution)/shard_map/convert_element_type | solution.py:58
  141.0 2.5 all-to-all-done.3
  143.5 5.5 %all-to-all-start.1 = ((bf16[8,128,1664]{2,0,1:T(8,128)(2,1)}), bf16[8,128,1664]{2,0,1:T(8,128)(2,1)}, u32[]{:S(2)}, u32[]{:S(2)}) async-start(bf16[8,128,1664]{2,0,1:T(8,128)(2,1)} %copy.79), calls=%async_computation.1 | async-start | bytes 6815744 | tf_op jit(solution)/shard_map/all_to_all | solution.py:59
  149.2 4.3 %fusion.9 = f32[8,128,128]{1,2,0:T(8,128)S(1)} fusion(bf16[8,128,1664]{1,2,0:T(8,128)(2,1)} %copy-done.5, bf16[8,16,8,1664]{3,2,0,1:T(8,128)(2,1)} %bitcast.2), kind=kOutput, calls=%fused_computation.17 | convolution fusion | flops 436207616 | bytes 7340032 | tf_op jit(solution)/shard_map/jit,jkt->jik/dot_general | solution.py:48
  154.8 72.4 %all-to-all-done.1 = bf16[8,128,1664]{2,0,1:T(8,128)(2,1)} async-done(((bf16[8,128,1664]{2,0,1:T(8,128)(2,1)}), bf16[8,128,1664]{2,0,1:T(8,128)(2,1)}, u32[]{:S(2)}, u32[]{:S(2)}) %all-to-all-start.1) | async-done | bytes 3407904 | tf_op jit(solution)/shard_map/all_to_all | solution.py:59
  227.3 2.6 %copy.81 = bf16[16,8,8,1664]{3,2,1,0:T(8,128)(2,1)S(1)} copy(bf16[16,8,8,1664]{3,1,2,0:T(8,128)(2,1)} %bitcast.8) | data formatting | bytes 6815744 | tf_op jit(solution)/shard_map/all_to_all | solution.py:59
  233.7 8.4 %all-to-all-start.4 = ((f32[2,8,128,128]{3,1,0,2:T(8,128)}), f32[2,8,128,128]{3,1,0,2:T(8,128)S(1)}, u32[]{:S(2)}, u32[]{:S(2)}) async-start(f32[2,8,128,128]{3,1,0,2:T(8,128)} %copy.99), calls=%async_computation.4 | async-start | bytes 2097152 | tf_op jit(solution)/shard_map/all_to_all | solution.py:16
  242.6 4.7 %fusion.1 = bf16[8,128,1664]{1,2,0:T(8,128)(2,1)S(1)} fusion(bf16[8,128,1664]{1,2,0:T(8,128)(2,1)} %copy.113, bf16[8,128,128]{2,1,0:T(8,128)(2,1)S(1)} %copy-done.4, bf16[128,8,1664]{2,1,0:T(8,128)(2,1)} %bitcast.82), kind=kOutput, calls=%fused_computation.5 | convolution fusion | flops 441319424 | bytes 10485760 | tf_op jit(solution)/shard_map/oit,ico->ict/dot_general | solution.py:60
  247.3 2.2 pad_maximum_fusion
  249.5 6.4 %copy.101 = bf16[8,128,2048]{2,1,0:T(8,128)(2,1)} copy(bf16[8,128,2048]{1,2,0:T(8,128)(2,1)} %pad_maximum_fusion) | data formatting | bytes 8388608
  256.0 3.3 %all-to-all-done.4 = f32[2,8,128,128]{3,1,0,2:T(8,128)S(1)} async-done(((f32[2,8,128,128]{3,1,0,2:T(8,128)}), f32[2,8,128,128]{3,1,0,2:T(8,128)S(1)}, u32[]{:S(2)}, u32[]{:S(2)}) %all-to-all-start.4) | async-done | bytes 1048608 | tf_op jit(solution)/shard_map/all_to_all | solution.py:16
  (40 shorter events, 12.0 us)
Async XLA Ops:
  0.6 50.4 %copy-start = (bf16[8,128,128]{2,1,0:T(8,128)(2,1)S(1)}, bf16[8,128,128]{2,1,0:T(8,128)(2,1)}, u32[]{:S(2)}) copy-start(bf16[8,128,128]{2,1,0:T(8,128)(2,1)} %param.6) | copy-start | bytes 786436
  0.6 13.1 %copy-start.4 = (bf16[8,128,128]{2,1,0:T(8,128)(2,1)S(1)}, bf16[8,128,128]{2,1,0:T(8,128)(2,1)}, u32[]{:S(2)}) copy-start(bf16[8,128,128]{2,1,0:T(8,128)(2,1)} %param.5) | copy-start | bytes 786436
  3.7 30.8 %all-to-all-start.2 = ((bf16[128,8,384]{2,1,0:T(8,128)(2,1)}), bf16[128,8,384]{2,1,0:T(8,128)(2,1)S(1)}, u32[]{:S(2)}, u32[]{:S(2)}) async-start(bf16[128,8,384]{2,1,0:T(8,128)(2,1)} %copy.85), calls=%async_computation.2 | async-start | bytes 1572864 | tf_op jit(solution)/shard_map/all_to_all | solution.py:39
  34.5 0.9 copy-start.8
  35.4 83.5 %all-to-all-start = ((bf16[128,8,1664]{2,1,0:T(8,128)(2,1)}), bf16[128,8,1664]{2,1,0:T(8,128)(2,1)}, u32[]{:S(2)}, u32[]{:S(2)}) async-start(bf16[128,8,1664]{2,1,0:T(8,128)(2,1)} %copy.76), calls=%async_computation | async-start | bytes 6815744 | tf_op jit(solution)/shard_map/all_to_all | solution.py:39
  40.7 4.1 %slice-start = ((bf16[8,128,2048]{2,1,0:T(8,128)(2,1)}), bf16[8,128,384]{2,1,0:T(8,128)(2,1)S(1)}, s32[]{:S(2)}) async-start(bf16[8,128,2048]{2,1,0:T(8,128)(2,1)} %param.7), calls=%async_computation.5 | async-start | bytes 1572864 | tf_op jit(solution)/shard_map/slice | solution.py:35
  45.2 5.9 %copy-start.6 = (bf16[8,128,384]{1,2,0:T(8,128)(2,1)}, bf16[8,128,384]{1,2,0:T(8,128)(2,1)S(1)}, u32[]{:S(2)}) copy-start(bf16[8,128,384]{1,2,0:T(8,128)(2,1)S(1)} %copy.114) | copy-start | bytes 2359300
  45.2 5.9 %copy-start.9 = (bf16[128,8,384]{2,1,0:T(8,128)(2,1)S(1)}, bf16[128,8,384]{2,1,0:T(8,128)(2,1)}, u32[]{:S(2)}) copy-start(bf16[128,8,384]{2,1,0:T(8,128)(2,1)} %copy-done.8) | copy-start | bytes 2359300
  118.9 24.7 %all-to-all-start.3 = ((bf16[8,128,384]{2,0,1:T(8,128)(2,1)}), bf16[8,128,384]{2,0,1:T(8,128)(2,1)S(1)}, u32[]{:S(2)}, u32[]{:S(2)}) async-start(bf16[8,128,384]{2,0,1:T(8,128)(2,1)} %copy.88), calls=%async_computation.3 | async-start | bytes 1572864 | tf_op jit(solution)/shard_map/all_to_all | solution.py:59
  130.6 1.7 copy-start.5
  143.5 83.7 %all-to-all-start.1 = ((bf16[8,128,1664]{2,0,1:T(8,128)(2,1)}), bf16[8,128,1664]{2,0,1:T(8,128)(2,1)}, u32[]{:S(2)}, u32[]{:S(2)}) async-start(bf16[8,128,1664]{2,0,1:T(8,128)(2,1)} %copy.79), calls=%async_computation.1 | async-start | bytes 6815744 | tf_op jit(solution)/shard_map/all_to_all | solution.py:59
  149.2 4.3 %copy-start.10 = (bf16[128,8,384]{2,1,0:T(8,128)(2,1)S(1)}, bf16[128,8,384]{2,1,0:T(8,128)(2,1)}, u32[]{:S(2)}) copy-start(bf16[128,8,384]{2,1,0:T(8,128)(2,1)} %copy-done.8) | copy-start | bytes 2359300
  227.3 3.2 %copy-start.3 = (bf16[8,128,2048]{2,1,0:T(8,128)(2,1)S(1)}, bf16[8,128,2048]{2,1,0:T(8,128)(2,1)}, u32[]{:S(2)}) copy-start(bf16[8,128,2048]{2,1,0:T(8,128)(2,1)} %param.4) | copy-start | bytes 12582916
  229.9 1.8 copy-start.2
  230.5 1.7 copy-start.11
  232.2 9.9 %copy-start.7 = (bf16[8,128,384]{1,2,0:T(8,128)(2,1)S(1)}, bf16[8,128,384]{1,2,0:T(8,128)(2,1)}, u32[]{:S(2)}) copy-start(bf16[8,128,384]{1,2,0:T(8,128)(2,1)} %copy-done.6) | copy-start | bytes 2359300
  233.7 25.5 %all-to-all-start.4 = ((f32[2,8,128,128]{3,1,0,2:T(8,128)}), f32[2,8,128,128]{3,1,0,2:T(8,128)S(1)}, u32[]{:S(2)}, u32[]{:S(2)}) async-start(f32[2,8,128,128]{3,1,0,2:T(8,128)} %copy.99), calls=%async_computation.4 | async-start | bytes 2097152 | tf_op jit(solution)/shard_map/all_to_all | solution.py:16
  247.3 12.7 %copy-start.1 = (bf16[8,128,128]{2,1,0:T(8,128)(2,1)S(1)}, bf16[8,128,128]{2,1,0:T(8,128)(2,1)}, u32[]{:S(2)}) copy-start(bf16[8,128,128]{2,1,0:T(8,128)(2,1)} %param.6) | copy-start | bytes 786436
